TPU v7x, 128 devices: a whole 4x4x4 slice. The times are simulated.
128 devices in a mesh: req: 8 (over y, x_hi), row: 4 (over x_lo, core), col: 4 (over z).
Axes of the slice: x: 4 (x_hi: 2, x_lo: 2; x = x_hi * 2 + x_lo), y: 4, z: 4, core: 2. Of those that a mesh axis runs over, the one named last changes fastest.
Arguments:
- text_embed: bfloat16 [6144, 4096], P(('req', 'col'), 'row')
- vis_embed: bfloat16 [4096, 4096], P(('req', 'col'), 'row')
- vis_segment: int32 [4096], P(('req', 'col')), may hold values from 0 to 20, never falling along the last dimension, each value on 1 to 256 neighbouring positions
- vis_valid: int32 [4096], P(('req', 'col')), may hold values 0 or 1
- vis_gain: bfloat16 [4096], P('row'), may hold values from 0.25 to 1.75
- vis_wq: bfloat16 [4096, 4096], P('row', 'col')
- vis_wk: bfloat16 [4096, 4096], P('row', 'col')
- vis_wv: bfloat16 [4096, 4096], P('row', 'col'), may hold values from -0.09375 to 0.09375
- vis_wo: bfloat16 [4096, 4096], P('col', 'row'), may hold values from -0.09375 to 0.09375
- dec_gain: bfloat16 [4096], P('row'), may hold values from 0.25 to 1.75
- dec_wq: bfloat16 [4096, 4096], P('row', 'col')
- dec_wk: bfloat16 [4096, 4096], P('row', 'col')
- dec_wv: bfloat16 [4096, 4096], P('row', 'col'), may hold values from -0.09375 to 0.09375
- dec_wo: bfloat16 [4096, 4096], P('col', 'row'), may hold values from -0.09375 to 0.09375
Outputs:
- hidden_out: bfloat16 [6144, 4096], P(('req', 'col'), 'row')
Inputs may be any that keep to these rules, and one draw needn't show every extreme that they name: `vis_segment`: images take consecutive slots in order, each 1 to 256 slots, one exactly 256.
All inputs are finite; a program needn't handle non-finite values. No bound on the sum of `vis_valid` on one device may be relied on, other than what follows from the above.
Results may differ from a plain program's by a relative error of at most 0.008.
Values may be sent and summed in bfloat16 or wider, within the bound.
No kernel may reach another device: no remote copies, remote signals or barrier semaphores. Data moves between devices by JAX's collectives and lax.ppermute only.
A program may use at most 192 MiB of HBM per device.

v0:
```python
import jax
import jax.numpy as jnp
from jax import lax
from jax.sharding import PartitionSpec as P

D = 4096
HD = 128
MAXIMG = 256


def with_halo(cells, sides, width):
    for axis, dim in sides:
        count = lax.axis_size(axis)
        ends = count - 1
        head = lax.slice_in_dim(cells, 0, width, axis=dim)
        tail = lax.slice_in_dim(cells, cells.shape[dim] - width, cells.shape[dim], axis=dim)
        cells = jnp.concatenate(
            [
                lax.ppermute(tail, axis, [(i, (i + 1) % count) for i in range(ends)]),
                cells,
                lax.ppermute(head, axis, [((i + 1) % count, i) for i in range(ends)]),
            ],
            axis=dim,
        )
    return cells


def passed_along(shard, axis, by):
    size = lax.axis_size(axis)
    pairs = [(i, i + by) for i in range(size) if 0 <= i + by < size]
    return lax.ppermute(shard, axis, pairs)


def norm_local(values, gain):
    floats = values.astype(jnp.float32)
    squares = jnp.sum(floats * floats, axis=-1)
    totals = lax.psum(squares, "row")
    factor = lax.rsqrt(totals / D + 1e-05)
    return (floats * factor[:, None] * gain.astype(jnp.float32)[None, :]).astype(jnp.bfloat16)


def gather_cols(values):
    return lax.all_gather(values, "col", axis=0, tiled=True)


def out_project(attended, weight):
    whole = lax.all_gather(attended, "row", axis=0, tiled=True)
    return lax.psum_scatter(
        jnp.dot(whole, weight, preferred_element_type=jnp.float32).astype(jnp.bfloat16),
        "col",
        scatter_dimension=0,
        tiled=True,
    ).astype(jnp.float32)


def split_heads(values):
    return values.reshape(values.shape[0], values.shape[1] // HD, HD)


def attend_block(queries, keys, values, allowed):
    query_heads = split_heads(queries)
    scores = jnp.einsum(
        "qhd,khd->hqk", query_heads, split_heads(keys), preferred_element_type=jnp.float32
    ) * HD ** (-0.5)
    scores = jnp.where(allowed[None], scores, -1e30)
    peak = jnp.max(scores, axis=-1, keepdims=True)
    weights = jnp.where(allowed[None], jnp.exp(scores - peak), 0.0)
    mass = jnp.sum(weights, axis=-1)
    summed = jnp.einsum(
        "hqk,khd->qhd",
        weights.astype(jnp.bfloat16),
        split_heads(values),
        preferred_element_type=jnp.float32,
    )
    result = summed / jnp.transpose(mass)[:, :, None]
    return result.reshape(queries.shape[0], queries.shape[1]).astype(jnp.bfloat16)


def fold_step(carry, query_heads, query_slots, key_heads, value_heads):
    peak, mass, accum = carry
    piece_slots = jnp.arange(key_heads.shape[0], dtype=jnp.int32)
    allowed = query_slots[:, None] >= piece_slots[None, :]
    scores = jnp.einsum(
        "qhd,khd->hqk", query_heads, key_heads, preferred_element_type=jnp.float32
    ) * HD ** (-0.5)
    scores = jnp.where(allowed[None], scores, -1e30)
    new_peak = jnp.maximum(peak, jnp.max(scores, axis=-1))
    weights = jnp.where(allowed[None], jnp.exp(scores - new_peak[:, :, None]), 0.0)
    summed = jnp.einsum(
        "hqk,khd->hqd",
        weights.astype(jnp.bfloat16),
        value_heads,
        preferred_element_type=jnp.float32,
    )
    return (new_peak, jnp.sum(weights, axis=-1), summed)


def start_state(head_count, query_count):
    return (
        jnp.full((head_count, query_count), -1e30, jnp.float32),
        jnp.zeros((head_count, query_count), jnp.float32),
        jnp.zeros((head_count, query_count, HD), jnp.float32),
    )


def head_project(values, weights):
    count = values.shape[0]
    row_count = lax.axis_size("row")
    width = weights[0].shape[1]
    parts = [
        jnp.dot(values, w, preferred_element_type=jnp.float32)
        .astype(jnp.bfloat16)
        .reshape(count, row_count, width // row_count)
        for w in weights
    ]
    stacked = jnp.stack(parts, axis=2).transpose(1, 0, 2, 3)
    stacked = stacked.reshape(row_count * count, len(weights) * (width // row_count))
    return lax.psum_scatter(stacked, "row", scatter_dimension=0, tiled=True)


def out_project_heads(attended, weight):
    row_count = lax.axis_size("row")
    whole = lax.all_gather(attended, "row", axis=0, tiled=False)
    shaped = weight.reshape(row_count, weight.shape[0] // row_count, weight.shape[1])
    summed = jnp.einsum("rtf,rfo->to", whole, shaped, preferred_element_type=jnp.float32)
    return lax.psum_scatter(
        summed.astype(jnp.bfloat16), "col", scatter_dimension=0, tiled=True
    ).astype(jnp.float32)


def per_device(
    text_embed,
    vis_embed,
    vis_segment,
    vis_valid,
    vis_gain,
    vis_wq,
    vis_wk,
    vis_wv,
    vis_wo,
    dec_gain,
    dec_wq,
    dec_wk,
    dec_wv,
    dec_wo,
):
    row_count = lax.axis_size("row")
    col_count = lax.axis_size("col")
    width = vis_wq.shape[1]
    local = width // row_count
    margin = MAXIMG - 1
    piece_ids = lax.all_gather(jnp.stack([vis_segment, vis_valid]), "col", axis=1, tiled=True)
    piece_len = piece_ids.shape[1]
    framed_ids = with_halo(piece_ids, (("req", 1),), margin)
    total_slots = piece_len * lax.axis_size("req")
    prompt_rows = text_embed.shape[0]
    prompt_total = prompt_rows * lax.axis_size("req") * col_count
    window_len = piece_len + 2 * margin
    window_start = lax.axis_index("req") * piece_len - margin
    window_index = jnp.arange(window_len, dtype=jnp.int32)
    key_slots = window_start + window_index
    inside = (key_slots >= 0) & (key_slots < total_slots)
    key_segment = framed_ids[0]
    key_valid = framed_ids[1]
    begins = jnp.concatenate([jnp.ones((1,), jnp.bool_), key_segment[1:] != key_segment[:-1]])
    begins = begins | (key_slots == 0)
    image_first = lax.cummax(jnp.where(begins, key_slots, window_start), axis=0)
    target_window = image_first * prompt_total // total_slots + key_slots - image_first
    vis_cols = gather_cols(norm_local(vis_embed, vis_gain))
    vis_proj = head_project(vis_cols, (vis_wq, vis_wk, vis_wv))
    vis_pairs = jnp.stack([vis_proj[:, local : 2 * local], vis_proj[:, 2 * local :]])
    framed = with_halo(vis_pairs, (("req", 1),), margin)
    query_local = margin + jnp.arange(piece_len, dtype=jnp.int32)
    query_slots = window_start + query_local
    query_segment = key_segment[query_local]
    seen = (
        inside[None, :]
        & (query_segment[:, None] == key_segment[None, :])
        & ((key_valid[None, :] == 1) | (query_slots[:, None] == key_slots[None, :]))
    )
    vis_att = attend_block(vis_proj[:, :local], framed[0], framed[1], seen)
    vis_out = (vis_embed.astype(jnp.float32) + out_project_heads(vis_att, vis_wo)).astype(
        jnp.bfloat16
    )
    device_place = lax.axis_index("req") * col_count + lax.axis_index("col")
    owned = device_place * prompt_rows + jnp.arange(prompt_rows, dtype=jnp.int32)
    slot_rows = vis_out.shape[0]
    following = passed_along(vis_out, ("req", "col"), -1)
    near_rows = jnp.concatenate([vis_out, following], axis=0)
    near_local = (
        margin + lax.axis_index("col") * slot_rows + jnp.arange(2 * slot_rows, dtype=jnp.int32)
    )
    near_slots = window_start + near_local
    present = near_slots < total_slots
    near_target = jnp.where(present, target_window[near_local], -1)
    near_valid = key_valid[near_local]
    onehot = ((owned[:, None] == near_target[None, :]) & (near_valid[None, :] == 1)).astype(
        jnp.bfloat16
    )
    carried = jnp.dot(onehot, near_rows, preferred_element_type=jnp.float32)
    mixed = (text_embed.astype(jnp.float32) + carried).astype(jnp.bfloat16)
    dec_cols = gather_cols(norm_local(mixed, dec_gain))
    dec_proj = head_project(dec_cols, (dec_wq, dec_wk, dec_wv))
    dec_rows = dec_cols.shape[0]
    dec_pairs = jnp.stack([dec_proj[:, local : 2 * local], dec_proj[:, 2 * local :]])
    piece = lax.all_gather(dec_pairs, "req", axis=1, tiled=True)
    token_slots = lax.axis_index("req") * dec_rows + jnp.arange(dec_rows, dtype=jnp.int32)
    all_slots = jnp.arange(piece.shape[1], dtype=jnp.int32)
    causal = token_slots[:, None] >= all_slots[None, :]
    dec_att = attend_block(dec_proj[:, :local], piece[0], piece[1], causal)
    return (mixed.astype(jnp.float32) + out_project_heads(dec_att, dec_wo)).astype(jnp.bfloat16)


def solution(mesh):
    return jax.shard_map(
        per_device,
        mesh=mesh,
        in_specs=(
            P(("req", "col"), "row"),
            P(("req", "col"), "row"),
            P(("req", "col")),
            P(("req", "col")),
            P("row"),
            P("row", "col"),
            P("row", "col"),
            P("row", "col"),
            P("col", "row"),
            P("row"),
            P("row", "col"),
            P("row", "col"),
            P("row", "col"),
            P("col", "row"),
        ),
        out_specs=P(("req", "col"), "row"),
        check_vma=False,
    )
```

profile of v0, /device:TPU:0, one launch (start us, length us, event | category | flops | bytes accessed | tf_op | source)
XLA Modules:
  0.0 563.6 jit_solution(1932380565323348486)
XLA Ops:
  7.8 7.0 %psum.14 = f32[128]{0:T(128)S(1)} all-reduce(f32[128]{0:T(128)S(1)} %fusion.34), channel_id=1, replica_groups=mesh['req'=8,'row'=4,'col'=4] {'row'}, use_global_device_ids=true, to_apply=%region_3.4 | all-reduce | flops 128 | bytes 1024 | tf_op jit(solution)/shard_map/psum | solution.py:37
  17.3 26.4 %all-gather.6.cloned.1.call-done = bf16[512,1024]{1,0:T(8,128)(2,1)} async-done(((bf16[128,1024]{1,0:T(8,128)(2,1)}), bf16[512,1024]{1,0:T(8,128)(2,1)}) %all-gather.6.cloned.1.call-update) | async-done | bytes 1048592 | tf_op jit(solution)/shard_map/all_gather | solution.py:43
  43.7 4.2 convolution_convert_fusion.3
  76.4 8.6 %all_gather.20 = s32[2,512]{1,0:T(2,128)S(1)} all-gather(s32[2,128]{1,0:T(2,128)S(1)} %pad_add_fusion.1), channel_id=1, replica_groups=mesh['req'=8,'row'=4,'col'=4] {'col'}, dimensions={1}, use_global_device_ids=true | all-gather | bytes 5120 | tf_op jit(solution)/shard_map/all_gather | solution.py:152
  85.0 4.9 collective-permute-start
  91.3 5.6 collective-permute-done.1
  97.0 16.1 %reduce-scatter.5.cloned.1.call-done = bf16[512,768]{0,1:T(8,128)(2,1)} async-done(((bf16[2048,768]{0,1:T(8,128)(2,1)}), bf16[512,768]{0,1:T(8,128)(2,1)}) %reduce-scatter.5.cloned.1.call-update) | async-done | bytes 786448 | tf_op jit(solution)/shard_map/reduce_scatter | solution.py:118
  115.1 5.3 collective-permute-start.2
  125.9 7.8 %collective-permute-done.3 = bf16[2,255,256]{1,2,0:T(8,128)(2,1)} collective-permute-done((bf16[2,255,256]{1,2,0:T(8,128)(2,1)}, bf16[2,255,256]{1,2,0:T(8,128)(2,1)}, u32[]{:S(2)}, u32[]{:S(2)}) %collective-permute-start.3) | collective-permute-done | bytes 261152 | tf_op jit(solution)/shard_map/ppermute | solution.py:21
  136.1 4.6 fusion.70
  144.0 21.4 %all-gather.8.cloned.1.call-done = bf16[4,512,256]{2,1,0:T(8,128)(2,1)} async-done(((bf16[1,512,256]{2,1,0:T(8,128)(2,1)}), bf16[4,512,256]{2,1,0:T(8,128)(2,1)}) %all-gather.8.cloned.1.call-update) | async-done | bytes 1048592 | tf_op jit(solution)/shard_map/all_gather | solution.py:123
  171.9 22.6 %reduce-scatter.7.cloned.1.call-done = bf16[128,1024]{1,0:T(8,128)(2,1)} async-done(((bf16[512,1024]{1,0:T(8,128)(2,1)}), bf16[128,1024]{1,0:T(8,128)(2,1)}) %reduce-scatter.7.cloned.1.call-update) | async-done | bytes 262160 | tf_op jit(solution)/shard_map/reduce_scatter | solution.py:126
  198.2 5.6 collective-permute-done.4
  205.2 5.7 %psum.15 = f32[192]{0:T(256)S(1)} all-reduce(f32[192]{0:T(256)S(1)} %get-tuple-element.23), channel_id=1, replica_groups=mesh['req'=8,'row'=4,'col'=4] {'row'}, use_global_device_ids=true, to_apply=%region_9.10 | all-reduce | flops 192 | bytes 1536 | tf_op jit(solution)/shard_map/psum | solution.py:37
  212.0 30.4 %all-gather.10.cloned.1.call-done = bf16[768,1024]{1,0:T(8,128)(2,1)} async-done(((bf16[192,1024]{1,0:T(8,128)(2,1)}), bf16[768,1024]{1,0:T(8,128)(2,1)}) %all-gather.10.cloned.1.call-update) | async-done | bytes 1572880 | tf_op jit(solution)/shard_map/all_gather | solution.py:43
  242.5 5.0 convolution_convert_fusion
  251.3 4.2 copy.37
  255.6 5.0 convolution_convert_fusion.2
  264.5 4.2 copy.35
  268.7 5.0 convolution_convert_fusion.1
  277.6 4.2 copy.36
  281.8 6.0 %pad_maximum_fusion = bf16[768,4,3,256]{0,1,3,2:T(4,128)(2,1)S(1)} fusion(bf16[768,4,1,256]{0,1,3,2:T(4,128)(2,1)} %copy.37, bf16[768,4,1,256]{0,1,3,2:T(4,128)(2,1)} %copy.36, bf16[768,4,1,256]{0,1,3,2:T(4,128)(2,1)} %copy.35), kind=kLoop, calls=%fused_computation.14 | loop fusion | flops 4718592 | bytes 9437184 | tf_op jit(solution)/shard_map/stack | solution.py:116
  291.0 49.6 %reduce-scatter.9.cloned.1.call-done = bf16[768,768]{0,1:T(8,128)(2,1)} async-done(((bf16[3072,768]{0,1:T(8,128)(2,1)}), bf16[768,768]{0,1:T(8,128)(2,1)}) %reduce-scatter.9.cloned.1.call-update) | async-done | bytes 1179664 | tf_op jit(solution)/shard_map/reduce_scatter | solution.py:118
  343.2 5.7 %iota_compare_fusion = pred[768,6144]{1,0:T(8,128)(4,1)} fusion(s32[768]{0:T(1024)S(1)} %iota_add_fusion), kind=kLoop, calls=%fused_computation.12 | loop fusion | flops 4718592 | bytes 4721664 | tf_op jit(solution)/shard_map/ge | solution.py:209
  348.9 83.6 %all-gather.12.cloned.1.call-done = bf16[2,6144,256]{1,2,0:T(8,128)(2,1)} async-done(((bf16[2,768,256]{1,2,0:T(8,128)(2,1)}), bf16[2,6144,256]{1,2,0:T(8,128)(2,1)}) %all-gather.12.cloned.1.call-update) | async-done | bytes 6291472 | tf_op jit(solution)/shard_map/all_gather | solution.py:206
  432.5 5.4 fusion.64
  437.9 14.7 %fusion.72 = f32[2,768,6144]{2,1,0:T(8,128)} fusion(bf16[768,2,128]{0,2,1:T(8,128)(2,1)S(1)} %bitcast.96, bf16[6144,2,128]{0,2,1:T(8,128)(2,1)S(1)} %bitcast.90), kind=kOutput, calls=%fused_computation.120 | convolution fusion | flops 2415919104 | bytes 41287680 | tf_op jit(solution)/shard_map/qhd,khd->hqk/dot_general | solution.py:62
  452.7 36.8 %fusion.71 = (f32[2,768]{1,0:T(2,128)S(1)}, bf16[2,768,6144]{2,1,0:T(8,128)(2,1)}) fusion(f32[2,768,6144]{2,1,0:T(8,128)} %fusion.72, pred[768,6144]{1,0:T(8,128)(4,1)S(1)} %bitcast.94), kind=kOutput, calls=%fused_computation.119 | output fusion | flops 75503616 | bytes 61347840 | tf_op jit(solution)/shard_map/sub | solution.py:67
  489.5 10.4 %fusion.31 = bf16[768,2,128]{0,2,1:T(8,128)(2,1)S(1)} fusion(bf16[6144,2,128]{0,2,1:T(8,128)(2,1)} %bitcast.95, bf16[2,768,6144]{2,1,0:T(8,128)(2,1)} %get-tuple-element.26, f32[768,2]{0,1:T(2,128)S(1)} %bitcast.107), kind=kOutput, calls=%fused_computation.41 | convolution fusion | flops 2416312320 | bytes 22419456 | tf_op jit(solution)/shard_map/hqk,khd->qhd/dot_general | solution.py:69
  500.9 22.7 %all-gather.14.cloned.1.call-done = bf16[4,768,256]{2,1,0:T(8,128)(2,1)} async-done(((bf16[1,768,256]{2,1,0:T(8,128)(2,1)}), bf16[4,768,256]{2,1,0:T(8,128)(2,1)}) %all-gather.14.cloned.1.call-update) | async-done | bytes 1572880 | tf_op jit(solution)/shard_map/all_gather | solution.py:123
  523.6 4.4 bitcast_convert_fusion
  528.0 27.0 %reduce-scatter.11.cloned.1.call-done = bf16[192,1024]{1,0:T(8,128)(2,1)} async-done(((bf16[768,1024]{1,0:T(8,128)(2,1)}), bf16[192,1024]{1,0:T(8,128)(2,1)}) %reduce-scatter.11.cloned.1.call-update) | async-done | bytes 393232 | tf_op jit(solution)/shard_map/reduce_scatter | solution.py:126
  (101 shorter events, 79.6 us)
Async XLA Ops:
  6.5 517.1 %copy-start = (bf16[1024,1024]{1,0:T(8,128)(2,1)S(1)}, bf16[1024,1024]{1,0:T(8,128)(2,1)}, u32[]{:S(2)}) copy-start(bf16[1024,1024]{1,0:T(8,128)(2,1)} %param.27) | copy-start | bytes 6291460
  6.5 37.1 %all-gather.6.cloned.1.call-start = ((), (), s32[]{:S(2)}) async-start(), calls=%async_computation.4 | async-start | bytes 1310720 | tf_op jit(solution)/shard_map/all_gather | solution.py:43
  17.2 95.9 %reduce-scatter.5.cloned.1.call-start = ((), (), s32[]{:S(2)}) async-start(), calls=%async_computation.5 | async-start | bytes 3932160 | tf_op jit(solution)/shard_map/reduce_scatter | solution.py:118
  75.7 0.7 copy-start.3
  75.7 0.7 copy-start.4
  75.7 89.7 %all-gather.8.cloned.1.call-start = ((), (), s32[]{:S(2)}) async-start(), calls=%async_computation.6 | async-start | bytes 1310720 | tf_op jit(solution)/shard_map/all_gather | solution.py:123
  85.0 6.3 %collective-permute-start = (s32[2,255]{1,0:T(2,128)S(1)}, s32[2,255]{1,0:T(2,128)S(1)}, u32[]{:S(2)}, u32[]{:S(2)}) collective-permute-start(s32[2,255]{1,0:T(2,128)S(1)} %get-tuple-element.19), channel_id=1, source_target_pairs={{0,16},{16,32},{32,48},{48,64},{64,80},{80,96},{96,112},{1,17},{17... | collective-permute-start | bytes 6128 | tf_op jit(solution)/shard_map/ppermute | solution.py:19
  89.9 7.0 %collective-permute-start.1 = (s32[2,255]{1,0:T(2,128)S(1)}, s32[2,255]{1,0:T(2,128)S(1)}, u32[]{:S(2)}, u32[]{:S(2)}) collective-permute-start(s32[2,255]{1,0:T(2,128)S(1)} %get-tuple-element.20), channel_id=1, source_target_pairs={{16,0},{32,16},{48,32},{64,48},{80,64},{96,80},{112,96},{17,1},{33... | collective-permute-start | bytes 6128 | tf_op jit(solution)/shard_map/ppermute | solution.py:21
  115.1 10.8 %collective-permute-start.2 = (bf16[2,255,256]{1,2,0:T(8,128)(2,1)}, bf16[2,255,256]{1,2,0:T(8,128)(2,1)}, u32[]{:S(2)}, u32[]{:S(2)}) collective-permute-start(bf16[2,255,256]{1,2,0:T(8,128)(2,1)} %get-tuple-element.15), channel_id=1, source_target_pairs={{0,16},{16,32},{32,48},{48,64},{64,80},{80,96},{96,112},{1,17},{17... | collective-permute-start | bytes 783368 | tf_op jit(solution)/shard_map/ppermute | solution.py:19
  120.5 13.3 %collective-permute-start.3 = (bf16[2,255,256]{1,2,0:T(8,128)(2,1)}, bf16[2,255,256]{1,2,0:T(8,128)(2,1)}, u32[]{:S(2)}, u32[]{:S(2)}) collective-permute-start(bf16[2,255,256]{1,2,0:T(8,128)(2,1)} %get-tuple-element.16), channel_id=1, source_target_pairs={{16,0},{32,16},{48,32},{64,48},{80,64},{96,80},{112,96},{17,1},{33... | collective-permute-start | bytes 783368 | tf_op jit(solution)/shard_map/ppermute | solution.py:21
  144.0 50.5 %reduce-scatter.7.cloned.1.call-start = ((), (), s32[]{:S(2)}) async-start(), calls=%async_computation.7 | async-start | bytes 1310720 | tf_op jit(solution)/shard_map/reduce_scatter | solution.py:126
  165.5 4.3 copy-start.2
  169.6 24.9 %copy-start.1 = (bf16[128,1024]{1,0:T(8,128)(2,1)S(1)}, bf16[128,1024]{1,0:T(8,128)(2,1)}, u32[]{:S(2)}) copy-start(bf16[128,1024]{1,0:T(8,128)(2,1)} %param.15) | copy-start | bytes 786436
  169.7 72.8 %all-gather.10.cloned.1.call-start = ((), (), s32[]{:S(2)}) async-start(), calls=%async_computation.8 | async-start | bytes 1966080 | tf_op jit(solution)/shard_map/all_gather | solution.py:43
  195.5 8.3 %collective-permute-start.4 = (bf16[128,1024]{1,0:T(8,128)(2,1)S(1)}, bf16[128,1024]{1,0:T(8,128)(2,1)S(1)}, u32[]{:S(2)}, u32[]{:S(2)}) collective-permute-start(bf16[128,1024]{1,0:T(8,128)(2,1)S(1)} %fusion.37), channel_id=1, source_target_pairs={{1,0},{2,1},{3,2},{16,3},{17,16},{18,17},{19,18},{32,19},{33,32},{... | collective-permute-start | bytes 786440 | tf_op jit(solution)/shard_map/ppermute | solution.py:31
  211.8 128.8 %reduce-scatter.9.cloned.1.call-start = ((), (), s32[]{:S(2)}) async-start(), calls=%async_computation.9 | async-start | bytes 5898240 | tf_op jit(solution)/shard_map/reduce_scatter | solution.py:118
  291.0 141.6 %all-gather.12.cloned.1.call-start = ((), (), s32[]{:S(2)}) async-start(), calls=%async_computation.10 | async-start | bytes 7077888 | tf_op jit(solution)/shard_map/all_gather | solution.py:206
  342.9 180.7 %all-gather.14.cloned.1.call-start = ((), (), s32[]{:S(2)}) async-start(), calls=%async_computation.11 | async-start | bytes 1966080 | tf_op jit(solution)/shard_map/all_gather | solution.py:123
  432.5 20.1 %slice-start = ((s8[4718592]{0:T(1024)(128)(4,1)}), s8[4194304]{0:T(1024)(128)(4,1)S(1)}, s32[]{:S(2)}) async-start(s8[4718592]{0:T(1024)(128)(4,1)} %bitcast.93), calls=%async_computation.13 | async-start | bytes 8388608
  437.9 14.7 %slice-start.1 = ((s8[4718592]{0:T(1024)(128)(4,1)}), s8[524288]{0:T(1024)(128)(4,1)S(1)}, s32[]{:S(2)}) async-start(s8[4718592]{0:T(1024)(128)(4,1)} %bitcast.93), calls=%async_computation.14 | async-start | bytes 1048576
  500.9 54.2 %reduce-scatter.11.cloned.1.call-start = ((), (), s32[]{:S(2)}) async-start(), calls=%async_computation.12 | async-start | bytes 1966080 | tf_op jit(solution)/shard_map/reduce_scatter | solution.py:126
Sparse Core Ops, SparseCore 0:
  17.4 26.2 all-gather.5
  75.9 37.1 reduce-scatter.4
  144.1 21.2 all-gather.7
  169.8 24.6 reduce-scatter.6
  211.9 30.5 all-gather.9
  291.1 49.5 reduce-scatter.8
  343.3 89.2 all-gather.11
  501.0 22.6 all-gather.13
  528.1 26.8 reduce-scatter.10
where the time goes:
time: 571 us; the launch traced here: 564 us
  waiting for transfers between devices  320 us (56%)
  matrix products  69.7 us (12%)
  other arithmetic  64.9 us (11%)
  local copies, waits for them, and re-layouts  59.1 us (10%)
  blocking collectives  21.2 us (4%)
  starting transfers between devices  15.2 us (3%)
  between operations  13.7 us (2%)
    all_gather x1, waiting for transfers between devices, per_device(): piece = lax.all_gather(dec_pairs, 'req', axis=1, tiled=True)  83.6 us
    reduce_scatter x2, waiting for transfers between devices, head_project(): return lax.psum_scatter(stacked, 'row', scatter_dimension=0, tiled=True)  65.7 us
    all_gather x2, waiting for transfers between devices, gather_cols(): return lax.all_gather(values, 'col', axis=0, tiled=True)  56.8 us
    reduce_scatter x2, waiting for transfers between devices, out_project_heads(): lax.psum_scatter(summed.astype(jnp.bfloat16), 'col', scatter_dimension=0,...  49.6 us
    all_gather x2, waiting for transfers between devices, out_project_heads(): whole = lax.all_gather(attended, 'row', axis=0, tiled=False)  44.1 us
    another operation x12, local copies, waits for them, and re-layouts, head_project(): stacked = jnp.stack(parts, axis=2).transpose(1, 0, 2, 3)  36.9 us
    sub x1, other arithmetic, attend_block(): weights = jnp.where(allowed[None], jnp.exp(scores - peak), 0.0)  36.8 us
    dot_general x6, matrix products, head_project(): jnp.dot(values, w, preferred_element_type=jnp.float32).astype(jnp.bfloat16)  27.6 us
  transfers between devices with their start and end apart: 14, of which 13 were waited for; matrix products, arithmetic and copies ran while one was open for 2% of the time, Pallas kernels for 0%

commit v1 on v0

--- a/solution.py
+++ b/solution.py
@@ -6,6 +6,13 @@
 D = 4096
 HD = 128
 MAXIMG = 256
+
+
+def swapped_in(x, name, dim):
+    count = lax.axis_size(name)
+    pieces = jnp.stack([x for _ in range(count)])
+    pieces = lax.all_to_all(pieces, name, split_axis=0, concat_axis=0)
+    return jnp.concatenate(pieces, axis=dim)
 
 
 def with_halo(cells, sides, width):
@@ -40,7 +47,7 @@
 
 
 def gather_cols(values):
-    return lax.all_gather(values, "col", axis=0, tiled=True)
+    return swapped_in(values, "col", 0)
 
 
 def out_project(attended, weight):

time: 571 us -> 553 us (0.968)
  waiting for transfers between devices: 320 us -> 262 us
  blocking collectives: 21.2 us -> 66.8 us
  matrix products: 69.7 us -> 62 us
    all_gather x2 -> x0, waiting for transfers between devices: 56.8 us -> none  [gather_cols(): return lax.all_gather(values, 'col', axis=0, tiled=True)]
    all_to_all x0 -> x2, blocking collectives: none -> 46 us  [swapped_in(): pieces = lax.all_to_all(pieces, name, split_axis=0, concat_axis=0)]
    dot_general x6, matrix products: 27.6 us -> 19.9 us  [head_project(): jnp.dot(values, w, preferred_element_type=jnp.float32).astype(jnp.bfloat16)]
  transfers between devices with their start and end apart: 14 -> 12, of which waited for: 13 -> 11; matrix products, arithmetic and copies ran while one was open for 2% -> 2% of each run, Pallas kernels for 0% -> 0%
where the time goes in v1:
time: 553 us; the launch traced here: 545 us
  waiting for transfers between devices  262 us (47%)
  blocking collectives  66.8 us (12%)
  other arithmetic  63.5 us (11%)
  matrix products  62 us (11%)
  local copies, waits for them, and re-layouts  61.6 us (11%)
  starting transfers between devices  15 us (3%)
  between operations  14.1 us (3%)
    all_gather x1, waiting for transfers between devices, per_device(): piece = lax.all_gather(dec_pairs, 'req', axis=1, tiled=True)  83.5 us
    reduce_scatter x2, waiting for transfers between devices, head_project(): return lax.psum_scatter(stacked, 'row', scatter_dimension=0, tiled=True)  65.2 us
    reduce_scatter x2, waiting for transfers between devices, out_project_heads(): lax.psum_scatter(summed.astype(jnp.bfloat16), 'col', scatter_dimension=0,...  49.6 us
    all_to_all x2, blocking collectives, swapped_in(): pieces = lax.all_to_all(pieces, name, split_axis=0, concat_axis=0)  46 us
    all_gather x2, waiting for transfers between devices, out_project_heads(): whole = lax.all_gather(attended, 'row', axis=0, tiled=False)  44.1 us
    another operation x12, local copies, waits for them, and re-layouts, head_project(): stacked = jnp.stack(parts, axis=2).transpose(1, 0, 2, 3)  36.8 us
    sub x1, other arithmetic, attend_block(): weights = jnp.where(allowed[None], jnp.exp(scores - peak), 0.0)  36.8 us
    dot_general x6, matrix products, head_project(): jnp.dot(values, w, preferred_element_type=jnp.float32).astype(jnp.bfloat16)  19.9 us
  transfers between devices with their start and end apart: 12, of which 11 were waited for; matrix products, arithmetic and copies ran while one was open for 2% of the time, Pallas kernels for 0%

profile of v1, /device:TPU:0, one launch (start us, length us, event | category | flops | bytes accessed | tf_op | source)
XLA Modules:
  0.0 545.4 jit_solution(15849691878108224303)
XLA Ops:
  7.8 7.0 %psum.14 = f32[128]{0:T(128)S(1)} all-reduce(f32[128]{0:T(128)S(1)} %fusion.34), channel_id=1, replica_groups=mesh['req'=8,'row'=4,'col'=4] {'row'}, use_global_device_ids=true, to_apply=%region_3.4 | all-reduce | flops 128 | bytes 1024 | tf_op jit(solution)/shard_map/psum | solution.py:44
  16.8 19.0 %all_to_all.10 = bf16[4,128,1024]{2,1,0:T(8,128)(2,1)S(1)} all-to-all(bf16[4,128,1024]{2,1,0:T(8,128)(2,1)S(1)} %stack.50), channel_id=1, replica_groups=mesh['req'=8,'row'=4,'col'=4] {'col'}, dimensions={0} | all-to-all | bytes 2097152 | tf_op jit(solution)/shard_map/all_to_all | solution.py:14
  43.3 4.3 convolution_convert_fusion.4
  58.3 4.2 pad_maximum_fusion.1
  65.8 8.1 %all_gather.14 = s32[2,512]{1,0:T(2,128)S(1)} all-gather(s32[2,128]{1,0:T(2,128)S(1)} %pad_add_fusion.1), channel_id=1, replica_groups=mesh['req'=8,'row'=4,'col'=4] {'col'}, dimensions={1}, use_global_device_ids=true | all-gather | bytes 5120 | tf_op jit(solution)/shard_map/all_gather | solution.py:159
  74.0 4.9 collective-permute-start
  80.3 5.8 %collective-permute-done.1 = s32[2,255]{1,0:T(2,128)S(1)} collective-permute-done((s32[2,255]{1,0:T(2,128)S(1)}, s32[2,255]{1,0:T(2,128)S(1)}, u32[]{:S(2)}, u32[]{:S(2)}) %collective-permute-start.1) | collective-permute-done | bytes 2072 | tf_op jit(solution)/shard_map/ppermute | solution.py:28
  86.2 15.4 %reduce-scatter.5.cloned.1.call-done = bf16[512,768]{0,1:T(8,128)(2,1)} async-done(((bf16[2048,768]{0,1:T(8,128)(2,1)}), bf16[512,768]{0,1:T(8,128)(2,1)}) %reduce-scatter.5.cloned.1.call-update) | async-done | bytes 786448 | tf_op jit(solution)/shard_map/reduce_scatter | solution.py:125
  103.7 5.3 collective-permute-start.2
  114.5 7.8 %collective-permute-done.3 = bf16[2,255,256]{1,2,0:T(8,128)(2,1)} collective-permute-done((bf16[2,255,256]{1,2,0:T(8,128)(2,1)}, bf16[2,255,256]{1,2,0:T(8,128)(2,1)}, u32[]{:S(2)}, u32[]{:S(2)}) %collective-permute-start.3) | collective-permute-done | bytes 261152 | tf_op jit(solution)/shard_map/ppermute | solution.py:28
  124.7 4.6 fusion.70
  132.6 21.4 %all-gather.4.cloned.1.call-done = bf16[4,512,256]{2,1,0:T(8,128)(2,1)} async-done(((bf16[1,512,256]{2,1,0:T(8,128)(2,1)}), bf16[4,512,256]{2,1,0:T(8,128)(2,1)}) %all-gather.4.cloned.1.call-update) | async-done | bytes 1048592 | tf_op jit(solution)/shard_map/all_gather | solution.py:130
  154.0 4.2 bitcast_convert_fusion.1
  160.4 22.6 %reduce-scatter.7.cloned.1.call-done = bf16[128,1024]{1,0:T(8,128)(2,1)} async-done(((bf16[512,1024]{1,0:T(8,128)(2,1)}), bf16[128,1024]{1,0:T(8,128)(2,1)}) %reduce-scatter.7.cloned.1.call-update) | async-done | bytes 262160 | tf_op jit(solution)/shard_map/reduce_scatter | solution.py:133
  186.8 5.6 %collective-permute-done.4 = bf16[128,1024]{1,0:T(8,128)(2,1)S(1)} collective-permute-done((bf16[128,1024]{1,0:T(8,128)(2,1)S(1)}, bf16[128,1024]{1,0:T(8,128)(2,1)S(1)}, u32[]{:S(2)}, u32[]{:S(2)}) %collective-permute-start.4) | collective-permute-done | bytes 262176 | tf_op jit(solution)/shard_map/ppermute | solution.py:38
  193.7 5.7 %psum.15 = f32[192]{0:T(256)S(1)} all-reduce(f32[192]{0:T(256)S(1)} %get-tuple-element.23), channel_id=1, replica_groups=mesh['req'=8,'row'=4,'col'=4] {'row'}, use_global_device_ids=true, to_apply=%region_9.10 | all-reduce | flops 192 | bytes 1536 | tf_op jit(solution)/shard_map/psum | solution.py:44
  199.8 27.0 %all_to_all.11 = bf16[4,192,1024]{2,1,0:T(8,128)(2,1)S(1)} all-to-all(bf16[4,192,1024]{2,1,0:T(8,128)(2,1)S(1)} %stack.55), channel_id=1, replica_groups=mesh['req'=8,'row'=4,'col'=4] {'col'}, dimensions={0} | all-to-all | bytes 3145728 | tf_op jit(solution)/shard_map/all_to_all | solution.py:14
  234.8 4.2 copy.37
  239.0 5.2 convolution_convert_fusion.1
  251.0 4.2 copy.35
  259.1 4.2 copy.36
  263.3 6.0 %pad_maximum_fusion = bf16[768,4,3,256]{0,1,3,2:T(4,128)(2,1)S(1)} fusion(bf16[768,4,1,256]{0,1,3,2:T(4,128)(2,1)} %copy.37, bf16[768,4,1,256]{0,1,3,2:T(4,128)(2,1)} %copy.36, bf16[768,4,1,256]{0,1,3,2:T(4,128)(2,1)} %copy.35), kind=kLoop, calls=%fused_computation.14 | loop fusion | flops 4718592 | bytes 9437184 | tf_op jit(solution)/shard_map/stack | solution.py:123
  272.5 49.8 %reduce-scatter.9.cloned.1.call-done = bf16[768,768]{0,1:T(8,128)(2,1)} async-done(((bf16[3072,768]{0,1:T(8,128)(2,1)}), bf16[768,768]{0,1:T(8,128)(2,1)}) %reduce-scatter.9.cloned.1.call-update) | async-done | bytes 1179664 | tf_op jit(solution)/shard_map/reduce_scatter | solution.py:125
  324.8 5.7 %iota_compare_fusion = pred[768,6144]{1,0:T(8,128)(4,1)} fusion(s32[768]{0:T(1024)S(1)} %iota_add_fusion), kind=kLoop, calls=%fused_computation.12 | loop fusion | flops 4718592 | bytes 4721664 | tf_op jit(solution)/shard_map/ge | solution.py:216
  330.5 83.5 %all-gather.6.cloned.1.call-done = bf16[2,6144,256]{1,2,0:T(8,128)(2,1)} async-done(((bf16[2,768,256]{1,2,0:T(8,128)(2,1)}), bf16[2,6144,256]{1,2,0:T(8,128)(2,1)}) %all-gather.6.cloned.1.call-update) | async-done | bytes 6291472 | tf_op jit(solution)/shard_map/all_gather | solution.py:213
  414.0 5.4 fusion.64
  419.4 14.7 %fusion.72 = f32[2,768,6144]{2,1,0:T(8,128)} fusion(bf16[768,2,128]{0,2,1:T(8,128)(2,1)S(1)} %bitcast.98, bf16[6144,2,128]{0,2,1:T(8,128)(2,1)S(1)} %bitcast.92), kind=kOutput, calls=%fused_computation.120 | convolution fusion | flops 2415919104 | bytes 41287680 | tf_op jit(solution)/shard_map/qhd,khd->hqk/dot_general | solution.py:69
  434.2 36.8 %fusion.71 = (f32[2,768]{1,0:T(2,128)S(1)}, bf16[2,768,6144]{2,1,0:T(8,128)(2,1)}) fusion(f32[2,768,6144]{2,1,0:T(8,128)} %fusion.72, pred[768,6144]{1,0:T(8,128)(4,1)S(1)} %bitcast.96), kind=kOutput, calls=%fused_computation.119 | output fusion | flops 75503616 | bytes 61347840 | tf_op jit(solution)/shard_map/sub | solution.py:74
  471.0 10.4 %fusion.31 = bf16[768,2,128]{0,2,1:T(8,128)(2,1)S(1)} fusion(bf16[6144,2,128]{0,2,1:T(8,128)(2,1)} %bitcast.97, bf16[2,768,6144]{2,1,0:T(8,128)(2,1)} %get-tuple-element.26, f32[768,2]{0,1:T(2,128)S(1)} %bitcast.115), kind=kOutput, calls=%fused_computation.41 | convolution fusion | flops 2416312320 | bytes 22419456 | tf_op jit(solution)/shard_map/hqk,khd->qhd/dot_general | solution.py:76
  482.4 22.7 %all-gather.8.cloned.1.call-done = bf16[4,768,256]{2,1,0:T(8,128)(2,1)} async-done(((bf16[1,768,256]{2,1,0:T(8,128)(2,1)}), bf16[4,768,256]{2,1,0:T(8,128)(2,1)}) %all-gather.8.cloned.1.call-update) | async-done | bytes 1572880 | tf_op jit(solution)/shard_map/all_gather | solution.py:130
  505.1 4.4 bitcast_convert_fusion
  509.5 27.0 %reduce-scatter.11.cloned.1.call-done = bf16[192,1024]{1,0:T(8,128)(2,1)} async-done(((bf16[768,1024]{1,0:T(8,128)(2,1)}), bf16[192,1024]{1,0:T(8,128)(2,1)}) %reduce-scatter.11.cloned.1.call-update) | async-done | bytes 393232 | tf_op jit(solution)/shard_map/reduce_scatter | solution.py:133
  (115 shorter events, 74.3 us)
Async XLA Ops:
  6.5 498.5 %copy-start = (bf16[1024,1024]{1,0:T(8,128)(2,1)S(1)}, bf16[1024,1024]{1,0:T(8,128)(2,1)}, u32[]{:S(2)}) copy-start(bf16[1024,1024]{1,0:T(8,128)(2,1)} %param.27) | copy-start | bytes 6291460
  6.5 95.1 %reduce-scatter.5.cloned.1.call-start = ((), (), s32[]{:S(2)}) async-start(), calls=%async_computation.6 | async-start | bytes 3932160 | tf_op jit(solution)/shard_map/reduce_scatter | solution.py:125
  14.7 22.1 %copy-start.9 = (bf16[1024,1024]{1,0:T(8,128)(2,1)S(1)}, bf16[1024,1024]{1,0:T(8,128)(2,1)}, u32[]{:S(2)}) copy-start(bf16[1024,1024]{1,0:T(8,128)(2,1)} %param.21) | copy-start | bytes 6291460
  35.8 1.0 copy-start.4
  43.2 4.3 copy-start.5
  43.3 4.3 copy-start.10
  65.1 0.7 copy-start.7
  65.1 0.7 copy-start.8
  65.2 88.8 %all-gather.4.cloned.1.call-start = ((), (), s32[]{:S(2)}) async-start(), calls=%async_computation.7 | async-start | bytes 1310720 | tf_op jit(solution)/shard_map/all_gather | solution.py:130
  74.0 6.3 %collective-permute-start = (s32[2,255]{1,0:T(2,128)S(1)}, s32[2,255]{1,0:T(2,128)S(1)}, u32[]{:S(2)}, u32[]{:S(2)}) collective-permute-start(s32[2,255]{1,0:T(2,128)S(1)} %get-tuple-element.19), channel_id=1, source_target_pairs={{0,16},{16,32},{32,48},{48,64},{64,80},{80,96},{96,112},{1,17},{17... | collective-permute-start | bytes 6128 | tf_op jit(solution)/shard_map/ppermute | solution.py:26
  79.0 7.2 %collective-permute-start.1 = (s32[2,255]{1,0:T(2,128)S(1)}, s32[2,255]{1,0:T(2,128)S(1)}, u32[]{:S(2)}, u32[]{:S(2)}) collective-permute-start(s32[2,255]{1,0:T(2,128)S(1)} %get-tuple-element.20), channel_id=1, source_target_pairs={{16,0},{32,16},{48,32},{64,48},{80,64},{96,80},{112,96},{17,1},{33... | collective-permute-start | bytes 6128 | tf_op jit(solution)/shard_map/ppermute | solution.py:28
  103.7 10.8 %collective-permute-start.2 = (bf16[2,255,256]{1,2,0:T(8,128)(2,1)}, bf16[2,255,256]{1,2,0:T(8,128)(2,1)}, u32[]{:S(2)}, u32[]{:S(2)}) collective-permute-start(bf16[2,255,256]{1,2,0:T(8,128)(2,1)} %get-tuple-element.15), channel_id=1, source_target_pairs={{0,16},{16,32},{32,48},{48,64},{64,80},{80,96},{96,112},{1,17},{17... | collective-permute-start | bytes 783368 | tf_op jit(solution)/shard_map/ppermute | solution.py:26
  109.0 13.3 %collective-permute-start.3 = (bf16[2,255,256]{1,2,0:T(8,128)(2,1)}, bf16[2,255,256]{1,2,0:T(8,128)(2,1)}, u32[]{:S(2)}, u32[]{:S(2)}) collective-permute-start(bf16[2,255,256]{1,2,0:T(8,128)(2,1)} %get-tuple-element.16), channel_id=1, source_target_pairs={{16,0},{32,16},{48,32},{64,48},{80,64},{96,80},{112,96},{17,1},{33... | collective-permute-start | bytes 783368 | tf_op jit(solution)/shard_map/ppermute | solution.py:28
  132.6 50.5 %reduce-scatter.7.cloned.1.call-start = ((), (), s32[]{:S(2)}) async-start(), calls=%async_computation.8 | async-start | bytes 1310720 | tf_op jit(solution)/shard_map/reduce_scatter | solution.py:133
  154.0 4.2 copy-start.6
  158.1 24.9 %copy-start.1 = (bf16[128,1024]{1,0:T(8,128)(2,1)S(1)}, bf16[128,1024]{1,0:T(8,128)(2,1)}, u32[]{:S(2)}) copy-start(bf16[128,1024]{1,0:T(8,128)(2,1)} %param.15) | copy-start | bytes 786436
  158.2 164.1 %reduce-scatter.9.cloned.1.call-start = ((), (), s32[]{:S(2)}) async-start(), calls=%async_computation.9 | async-start | bytes 5898240 | tf_op jit(solution)/shard_map/reduce_scatter | solution.py:125
  184.1 8.3 %collective-permute-start.4 = (bf16[128,1024]{1,0:T(8,128)(2,1)S(1)}, bf16[128,1024]{1,0:T(8,128)(2,1)S(1)}, u32[]{:S(2)}, u32[]{:S(2)}) collective-permute-start(bf16[128,1024]{1,0:T(8,128)(2,1)S(1)} %fusion.37), channel_id=1, source_target_pairs={{1,0},{2,1},{3,2},{16,3},{17,16},{18,17},{19,18},{32,19},{33,32},{... | collective-permute-start | bytes 786440 | tf_op jit(solution)/shard_map/ppermute | solution.py:38
  199.5 28.4 %copy-start.11 = (bf16[1024,1024]{1,0:T(8,128)(2,1)S(1)}, bf16[1024,1024]{1,0:T(8,128)(2,1)}, u32[]{:S(2)}) copy-start(bf16[1024,1024]{1,0:T(8,128)(2,1)} %param.26) | copy-start | bytes 6291460
  226.8 1.2 copy-start.2
  239.0 5.2 copy-start.3
  239.0 5.2 copy-start.12
  272.5 141.5 %all-gather.6.cloned.1.call-start = ((), (), s32[]{:S(2)}) async-start(), calls=%async_computation.10 | async-start | bytes 7077888 | tf_op jit(solution)/shard_map/all_gather | solution.py:213
  324.5 180.5 %all-gather.8.cloned.1.call-start = ((), (), s32[]{:S(2)}) async-start(), calls=%async_computation.11 | async-start | bytes 1966080 | tf_op jit(solution)/shard_map/all_gather | solution.py:130
  414.0 20.2 %slice-start = ((s8[4718592]{0:T(1024)(128)(4,1)}), s8[4194304]{0:T(1024)(128)(4,1)S(1)}, s32[]{:S(2)}) async-start(s8[4718592]{0:T(1024)(128)(4,1)} %bitcast.95), calls=%async_computation.13 | async-start | bytes 8388608
  419.4 14.7 %slice-start.1 = ((s8[4718592]{0:T(1024)(128)(4,1)}), s8[524288]{0:T(1024)(128)(4,1)S(1)}, s32[]{:S(2)}) async-start(s8[4718592]{0:T(1024)(128)(4,1)} %bitcast.95), calls=%async_computation.14 | async-start | bytes 1048576
  482.3 54.2 %reduce-scatter.11.cloned.1.call-start = ((), (), s32[]{:S(2)}) async-start(), calls=%async_computation.12 | async-start | bytes 1966080 | tf_op jit(solution)/shard_map/reduce_scatter | solution.py:133
Sparse Core Ops, SparseCore 0:
  65.3 36.3 reduce-scatter.4
  132.7 21.2 all-gather.3
  158.3 24.6 reduce-scatter.6
  272.6 49.6 reduce-scatter.8
  324.7 89.2 all-gather.5
  482.4 22.6 all-gather.7
  509.6 26.8 reduce-scatter.10
